TPU v7x, 32 devices: a whole 2x2x4 slice. The times are simulated.
32 devices in a mesh: energy: 4 (over z), atom: 8 (over y, x, core).
Axes of the slice: x: 2, y: 2, z: 4, core: 2. Of those that a mesh axis runs over, the one named last changes fastest.
Arguments:
- t_mats: bfloat16 [4, 16, 2048], P('energy', 'atom'), may hold values from -0.75 to 0.75
- struct_table: bfloat16 [4, 64, 2048], P('energy'), may hold values from -0.359375 to 0.359375
- zone_atoms: int32 [16, 64], P('atom'), may hold values from 0 to 15, as said below
- zone_size: int32 [16], P('atom'), may hold values from 32 to 64
- pair_index: int32 [16, 384], P('atom'), may hold values from 0 to 63
- zone_link: int32 [16, 384], P('atom'), may hold values from 0 to 63
- weights: float32 [4, 2], P('energy'), may hold values from -1 to 1
Outputs:
- green: float32 [16, 2048], P('atom')
Inputs may be any that keep to these rules, and one draw needn't show every extreme that they name: Atom g is owned by index g // 2 of the atom axis; zone_atoms[g, 0] is g; the owner of every member of atom g's zone lies -4 to 3 steps from g's owner along the atom axis, counted around the axis, and both extreme offsets occur in every zone; members may repeat (periodic images).
All inputs are finite; a program needn't handle non-finite values.
Results may differ from a plain program's by a relative error of at most 0.003.
Values may be sent and summed in bfloat16 or wider, within the bound.
No kernel may reach another device: no remote copies, remote signals or barrier semaphores. Data moves between devices by JAX's collectives and lax.ppermute only.
A program may use at most 128 MiB of HBM per device.

v0:
```python
import jax
import jax.numpy as jnp
from jax import lax
from jax.sharding import PartitionSpec as P

L = 32
Z = 64
NB = 6
ITERS = 3


def real_form(block):
    parts = block.reshape(block.shape[:-1] + (2, L, L))
    real_part = parts[..., 0, :, :]
    imag_part = parts[..., 1, :, :]
    top_rows = jnp.concatenate([real_part, -imag_part], axis=-1)
    bottom_rows = jnp.concatenate([imag_part, real_part], axis=-1)
    return jnp.concatenate([top_rows, bottom_rows], axis=-2)


def scatter_terms(couplings, gathered, pattern):
    products = jnp.einsum(pattern, couplings, gathered, preferred_element_type=jnp.float32)
    real_part = products[..., 0, 0, :, :] - products[..., 1, 1, :, :]
    imag_part = products[..., 1, 0, :, :] + products[..., 0, 1, :, :]
    return jnp.concatenate([real_part, imag_part], axis=-2)


def take_links(column_parts, link_rows):
    return jax.vmap(
        lambda member_col, member_links: member_col[:, member_links], in_axes=(1, 0), out_axes=1
    )(column_parts, link_rows)


def solve_zones(zone_block, couplings_flat, links):
    e_dev, a_dev = (zone_block.shape[0], zone_block.shape[1])
    t_real = real_form(zone_block)
    couplings = couplings_flat.reshape(e_dev, a_dev, Z, NB, 2, L, L)
    start_block = t_real[:, :, 0, :, :L].astype(jnp.float32)
    start = jnp.zeros((e_dev, a_dev, Z, 2 * L, L), jnp.float32).at[:, :, 0].set(start_block)
    column = start
    for repeat in range(ITERS - 1):
        column_parts = column.astype(jnp.bfloat16).reshape(e_dev, a_dev, Z, 2, L, L)
        gathered = take_links(column_parts, links).reshape(e_dev, a_dev, Z, NB, 2, L, L)
        coupled = scatter_terms(couplings, gathered, "eganpij,eganqjk->egapqik").astype(
            jnp.bfloat16
        )
        column = (
            jnp.einsum("egaij,egajk->egaik", t_real, coupled, preferred_element_type=jnp.float32)
            + start
        )
    column_parts = column.astype(jnp.bfloat16).reshape(e_dev, a_dev, Z, 2, L, L)
    gathered = take_links(column_parts, links[:, :NB])
    coupled = scatter_terms(couplings[:, :, 0], gathered, "egnpij,egnqjk->egpqik").astype(
        jnp.bfloat16
    )
    return (
        jnp.einsum("egij,egjk->egik", t_real[:, :, 0], coupled, preferred_element_type=jnp.float32)
        + start_block
    )


def body(t_mats, struct_table, zone_atoms, zone_size, pair_index, zone_link, weights):
    e_dev, a_dev, block_flat = t_mats.shape
    window = lax.all_gather(t_mats, "atom", axis=1, tiled=True)
    present = jnp.arange(Z, dtype=jnp.int32)[None, :] < zone_size[:, None]
    zone_block = jnp.where(
        present[None, :, :, None], window[:, zone_atoms], jnp.zeros((), jnp.bfloat16)
    )
    couplings_flat = struct_table[:, pair_index]
    diagonal = solve_zones(zone_block, couplings_flat, zone_link)
    real_rows = diagonal[:, :, :L, :].reshape(e_dev, a_dev, L * L)
    imag_rows = diagonal[:, :, L:, :].reshape(e_dev, a_dev, L * L)
    w_real = weights[:, 0][:, None, None]
    w_imag = weights[:, 1][:, None, None]
    green_real = jnp.sum(w_real * real_rows - w_imag * imag_rows, axis=0)
    green_imag = jnp.sum(w_real * imag_rows + w_imag * real_rows, axis=0)
    local_green = jnp.concatenate([green_real, green_imag], axis=-1)
    return lax.psum(local_green, "energy")


def solution(mesh):
    return jax.shard_map(
        body,
        mesh=mesh,
        in_specs=(
            P("energy", "atom", None),
            P("energy", None, None),
            P("atom", None),
            P("atom"),
            P("atom", None),
            P("atom", None),
            P("energy", None),
        ),
        out_specs=P("atom", None),
        check_vma=False,
    )
```

profile of v0, /device:TPU:0, one launch (start us, length us, event | category | flops | bytes accessed | tf_op | source)
XLA Modules:
  0.0 153.0 jit_solution(8475652753170242469)
XLA Ops:
  0.0 0.8 copy.91
  0.8 10.7 %all_gather.3 = bf16[1,16,2048]{2,0,1:T(2,128)(2,1)S(1)} all-gather(bf16[1,2,2048]{2,0,1:T(2,128)(2,1)S(1)} %copy.91), channel_id=1, replica_groups=mesh['energy'=4,'atom'=8] {'atom'}, dimensions={1}, use_global_device_ids=true | all-gather | bytes 73728 | tf_op jit(solution)/shard_map/all_gather | solution.py:64
  11.5 0.7 compare_select_fusion.3
  12.3 0.9 gather_fusion
  13.9 2.0 %copy.93 = bf16[1,2,64,2,32,32]{5,4,2,1,3,0:T(8,128)(2,1)S(1)} copy(bf16[1,2,64,2,32,32]{2,1,5,4,3,0:T(2,128)(2,1)S(1)} %gather.18) | data formatting | bytes 1048576 | tf_op jit(solution)/shard_map/gather | solution.py:67
  16.7 1.2 maximum_maximum_fusion
  18.4 0.8 copy-done.4
  19.3 9.2 %gather_fusion.2 = bf16[768,2,32,32]{3,2,1,0:T(8,128)(2,1)} fusion(bf16[2,64,2,32,32]{4,3,2,1,0:T(8,128)(2,1)S(1)} %bitcast.153, s32[768]{0:T(1024)S(1)} %reshape.305), kind=kCustom, calls=%fused_computation.2 | custom fusion | bytes 6297600 | tf_op jit(solution)/shard_map/vmap()/gather | solution.py:30
  28.5 3.4 %gather_fusion.1 = bf16[768,2048]{1,0:T(8,128)(2,1)S(1)} fusion(bf16[64,2048]{1,0:T(8,128)(2,1)S(1)} %bitcast.151, s32[1024]{0:T(1024)S(1)} %pad_clamp_fusion), kind=kCustom, calls=%fused_computation.1 | custom fusion | bytes 6294528 | tf_op jit(solution)/shard_map/gather | solution.py:69
  31.9 11.8 %reshape.277 = bf16[2,64,6,2,32,32]{5,4,3,2,1,0:T(8,128)(2,1)} reshape(bf16[768,2048]{1,0:T(8,128)(2,1)S(1)} %gather_fusion.1) | data formatting | bytes 6291456 | tf_op jit(solution)/shard_map/reshape.48
  43.7 17.2 %fusion.6 = f32[1,2,64,2,2,32,32]{5,6,3,4,2,1,0:T(8,128)} fusion(bf16[2,64,6,2,32,32,1]{5,4,3,2,1,0,6:T(8,128)(2,1)} %bitcast.155, bf16[2,64,6,2,32,32]{5,4,3,2,1,0:T(8,128)(2,1)} %reshape.277), kind=kOutput, calls=%fused_computation.11 | convolution fusion | flops 201326592 | bytes 8388608 | tf_op jit(solution)/shard_map/eganpij,eganqjk->egapqik/dot_general | solution.py:22
  60.9 2.7 %fusion.27 = bf16[2,64,32,32]{2,3,1,0:T(8,128)(2,1)S(1)} fusion(f32[1,2,64,2,2,32,32]{5,6,3,4,2,1,0:T(8,128)} %fusion.6), kind=kLoop, calls=%fused_computation.34 | loop fusion | flops 262144 | bytes 1310720 | tf_op jit(solution)/shard_map/sub | solution.py:23
  63.7 2.9 %fusion.28 = bf16[2,64,32,32]{2,3,1,0:T(8,128)(2,1)S(1)} fusion(f32[1,2,64,2,2,32,32]{5,6,3,4,2,1,0:T(8,128)} %fusion.6), kind=kLoop, calls=%fused_computation.35 | loop fusion | flops 262144 | bytes 1310720 | tf_op jit(solution)/shard_map/add | solution.py:24
  66.6 1.3 fusion.24
  67.9 1.3 copy-done.7
  70.0 1.8 %convert_element_type.37 = bf16[1,2,64,64,32]{3,4,2,1,0:T(8,128)(2,1)S(1)} convert(f32[1,2,64,64,32]{3,4,2,1,0:T(8,128)} %constant_dynamic-update-slice_fusion.1) | non-fusion elementwise | flops 262144 | bytes 1572864 | tf_op jit(solution)/shard_map/convert_element_type | solution.py:42
  71.8 1.2 copy.129
  73.0 9.4 %gather_fusion.3 = bf16[768,2,32,32]{3,2,1,0:T(8,128)(2,1)} fusion(bf16[2,64,2,32,32]{4,3,2,1,0:T(8,128)(2,1)S(1)} %bitcast.154, s32[768]{0:T(1024)S(1)} %reshape.305), kind=kCustom, calls=%fused_computation.3 | custom fusion | bytes 6297600 | tf_op jit(solution)/shard_map/vmap()/gather | solution.py:30
  82.4 17.2 %fusion.11 = f32[1,2,64,2,2,32,32]{5,6,3,4,2,1,0:T(8,128)} fusion(bf16[2,64,6,2,32,32,1]{5,4,3,2,1,0,6:T(8,128)(2,1)} %bitcast.156, bf16[2,64,6,2,32,32]{5,4,3,2,1,0:T(8,128)(2,1)} %reshape.277), kind=kOutput, calls=%fused_computation.12 | convolution fusion | flops 201326592 | bytes 8388608 | tf_op jit(solution)/shard_map/eganpij,eganqjk->egapqik/dot_general | solution.py:22
  99.6 2.7 %fusion.29 = bf16[2,64,32,32]{2,3,1,0:T(8,128)(2,1)S(1)} fusion(f32[1,2,64,2,2,32,32]{5,6,3,4,2,1,0:T(8,128)} %fusion.11), kind=kLoop, calls=%fused_computation.36 | loop fusion | flops 262144 | bytes 1310720 | tf_op jit(solution)/shard_map/sub | solution.py:23
  102.3 2.9 %fusion.30 = bf16[2,64,32,32]{2,3,1,0:T(8,128)(2,1)S(1)} fusion(f32[1,2,64,2,2,32,32]{5,6,3,4,2,1,0:T(8,128)} %fusion.11), kind=kLoop, calls=%fused_computation.37 | loop fusion | flops 262144 | bytes 1310720 | tf_op jit(solution)/shard_map/add | solution.py:24
  105.2 1.3 fusion.22
  106.5 1.3 copy-done.8
  108.0 0.6 constant_dynamic-update-slice_fusion
  108.6 2.8 %convert_element_type.38 = bf16[1,2,64,64,32]{3,4,2,1,0:T(8,128)(2,1)} convert(f32[1,2,64,64,32]{3,4,2,1,0:T(8,128)} %constant_dynamic-update-slice_fusion) | non-fusion elementwise | flops 262144 | bytes 1572864 | tf_op jit(solution)/shard_map/convert_element_type | solution.py:51
  111.4 2.9 %copy.134 = bf16[1,2,64,64,32]{4,3,2,1,0:T(8,128)(2,1)} copy(bf16[1,2,64,64,32]{3,4,2,1,0:T(8,128)(2,1)} %convert_element_type.38) | data formatting | bytes 1048576 | tf_op jit(solution)/shard_map/vmap()/transpose;reshape | solution.py:30
  114.4 2.9 %gather_fusion.4 = bf16[12,2,32,32]{3,2,1,0:T(8,128)(2,1)} fusion(bf16[2,64,2,32,32]{4,3,2,1,0:T(8,128)(2,1)} %bitcast.159, s32[12]{0:T(128)S(1)} %reshape.321), kind=kCustom, calls=%fused_computation.4 | custom fusion | bytes 98400 | tf_op jit(solution)/shard_map/vmap()/gather | solution.py:30
  117.4 11.6 %reshape.280 = bf16[1,2,64,6,2,32,32]{6,5,4,3,2,1,0:T(8,128)(2,1)} reshape(bf16[768,2048]{1,0:T(8,128)(2,1)S(1)} %copy-done.3) | data formatting | bytes 6291456 | tf_op jit(solution)/shard_map/reshape | solution.py:37
  129.0 1.3 convolution_bitcast_fusion
  130.3 1.0 fusion.26
  132.0 1.2 multiply_subtract_fusion
  133.4 19.6 %psum.7 = f32[2,2048]{1,0:T(2,128)} all-reduce(f32[2,2048]{1,0:T(2,128)S(1)} %pad_maximum_fusion), channel_id=1, replica_groups=mesh['energy'=4,'atom'=8] {'energy'}, use_global_device_ids=true, to_apply=%region_0.1 | all-reduce | flops 4096 | bytes 32768 | tf_op jit(solution)/shard_map/psum | solution.py:78
  (56 shorter events, 4.1 us)
Async XLA Ops:
  0.0 28.5 %copy-start = (bf16[1,64,2048]{2,1,0:T(8,128)(2,1)S(1)}, bf16[1,64,2048]{2,1,0:T(8,128)(2,1)}, u32[]{:S(2)}) copy-start(bf16[1,64,2048]{2,1,0:T(8,128)(2,1)} %param.10) | copy-start | bytes 786436
  13.5 2.4 %copy-start.12 = (s32[2]{0:T(128)S(1)}, s32[2]{0:T(128)}, u32[]{:S(2)}) copy-start(s32[2]{0:T(128)} %param.12) | copy-start | bytes 28
  17.9 1.4 copy-start.4
  17.9 1.4 copy-start.9
  19.3 9.2 %copy-start.10 = (s32[2,384]{1,0:T(2,128)S(1)}, s32[2,384]{1,0:T(2,128)}, u32[]{:S(2)}) copy-start(s32[2,384]{1,0:T(2,128)} %param.13) | copy-start | bytes 9220
  31.9 11.8 %copy-start.2 = (bf16[768,2048]{1,0:T(8,128)(2,1)}, bf16[768,2048]{1,0:T(8,128)(2,1)S(1)}, u32[]{:S(2)}) copy-start(bf16[768,2048]{1,0:T(8,128)(2,1)S(1)} %gather_fusion.1) | copy-start | bytes 9437188
  63.7 2.9 %copy-start.5 = (bf16[1,2,64,64,64]{4,3,2,1,0:T(8,128)(2,1)S(1)}, bf16[1,2,64,64,64]{4,3,2,1,0:T(8,128)(2,1)}, u32[]{:S(2)}) copy-start(bf16[1,2,64,64,64]{4,3,2,1,0:T(8,128)(2,1)} %copy-done.4) | copy-start | bytes 3145732
  67.9 1.3 copy-start.7
  102.3 2.9 %copy-start.6 = (bf16[1,2,64,64,64]{4,3,2,1,0:T(8,128)(2,1)S(1)}, bf16[1,2,64,64,64]{4,3,2,1,0:T(8,128)(2,1)}, u32[]{:S(2)}) copy-start(bf16[1,2,64,64,64]{4,3,2,1,0:T(8,128)(2,1)} %copy-done.4) | copy-start | bytes 3145732
  106.5 1.3 copy-start.8
  111.4 5.9 %copy-start.3 = (bf16[768,2048]{1,0:T(8,128)(2,1)S(1)}, bf16[768,2048]{1,0:T(8,128)(2,1)}, u32[]{:S(2)}) copy-start(bf16[768,2048]{1,0:T(8,128)(2,1)} %copy-done.2) | copy-start | bytes 9437188
  117.3 14.0 %copy-start.11 = (f32[1,2]{1,0:T(1,128)S(1)}, f32[1,2]{1,0:T(1,128)}, u32[]{:S(2)}) copy-start(f32[1,2]{1,0:T(1,128)} %param.15) | copy-start | bytes 28
  117.3 35.6 %copy-start.1 = (bf16[1,64,2048]{2,1,0:T(8,128)(2,1)S(1)}, bf16[1,64,2048]{2,1,0:T(8,128)(2,1)}, u32[]{:S(2)}) copy-start(bf16[1,64,2048]{2,1,0:T(8,128)(2,1)} %param.10) | copy-start | bytes 786436
where the time goes:
time: 153 us
  local copies, waits for them, and re-layouts  63.7 us (42%)
  matrix products  39.3 us (26%)
  blocking collectives  30.3 us (20%)
  other arithmetic  19.4 us (13%)
    dot_general x3, matrix products, scatter_terms(): jnp.einsum(pattern, couplings, gathered, preferred_element_type=jnp.float32)  35.7 us
    gather x5, local copies, waits for them, and re-layouts, take_links(): member_col[:, member_links]  21.5 us
    psum x1, blocking collectives, body(): return lax.psum(local_green, 'energy')  19.6 us
    another operation x3, local copies, waits for them, and re-layouts  11.8 us
    reshape x1, local copies, waits for them, and re-layouts, solve_zones(): couplings = couplings_flat.reshape(e_dev, a_dev, Z, NB, 2, L, L)  11.6 us
    all_gather x1, blocking collectives, body(): window = lax.all_gather(t_mats, 'atom', axis=1, tiled=True)  10.7 us
    add x3, other arithmetic, scatter_terms(): imag_part = products[..., 1, 0, :, :] + products[..., 0, 1, :, :]  5.8 us
    sub x3, other arithmetic, scatter_terms(): real_part = products[..., 0, 0, :, :] - products[..., 1, 1, :, :]  5.49 us

commit v1 on v0

--- a/solution.py
+++ b/solution.py
@@ -61,7 +61,24 @@
 
 def body(t_mats, struct_table, zone_atoms, zone_size, pair_index, zone_link, weights):
     e_dev, a_dev, block_flat = t_mats.shape
-    window = lax.all_gather(t_mats, "atom", axis=1, tiled=True)
+    devices, index, extent = (lax.axis_size("atom"), lax.axis_index("atom"), t_mats.shape[1])
+    right = [(i, (i + 1) % devices) for i in range(devices)]
+    behind = [(i, (i - 1) % devices) for i in range(devices)]
+    out = jnp.zeros((*t_mats.shape[:1], devices * extent, *t_mats.shape[1 + 1 :]), t_mats.dtype)
+    out = lax.dynamic_update_slice_in_dim(out, t_mats, index * extent, axis=1)
+    from_left = from_right = t_mats
+    half = devices // 2
+    for step in range(1, half + 1):
+        from_left = lax.ppermute(from_left, "atom", right)
+        out = lax.dynamic_update_slice_in_dim(
+            out, from_left, (index - step) % devices * extent, axis=1
+        )
+        if step < devices - half:
+            from_right = lax.ppermute(from_right, "atom", behind)
+            out = lax.dynamic_update_slice_in_dim(
+                out, from_right, (index + step) % devices * extent, axis=1
+            )
+    window = out
     present = jnp.arange(Z, dtype=jnp.int32)[None, :] < zone_size[:, None]
     zone_block = jnp.where(
         present[None, :, :, None], window[:, zone_atoms], jnp.zeros((), jnp.bfloat16)

time: 153 us -> 159 us (1.039)
  blocking collectives: 30.3 us -> 20.3 us
  starting transfers between devices: 0 us -> 8.66 us
  waiting for transfers between devices: 0 us -> 6.54 us
  other arithmetic: 19.4 us -> 21.3 us
    all_gather x1 -> x0, blocking collectives: 10.7 us -> none  [body(): window = lax.all_gather(t_mats, 'atom', axis=1, tiled=True)]
    ppermute x0 -> x7, starting transfers between devices: none -> 8.66 us  [the longest x3 8.17 us: body(): from_right = lax.ppermute(from_right, 'atom', behind)]
    ppermute x0 -> x7, waiting for transfers between devices: none -> 6.54 us  [the longest x4 6.48 us: body(): from_left = lax.ppermute(from_left, 'atom', right)]
    unnamed x30 -> x16, local copies, waits for them, and re-layouts: 4.5 us -> 4.24 us
  transfers between devices with their start and end apart: 0 -> 7, of which waited for: 0 -> 3; matrix products, arithmetic and copies ran while one was open for 0% -> 21% of each run, Pallas kernels for 0% -> 0%
where the time goes in v1:
time: 159 us
  local copies, waits for them, and re-layouts  63.1 us (40%)
  matrix products  38.4 us (24%)
  other arithmetic  21.3 us (13%)
  blocking collectives  20.3 us (13%)
  starting transfers between devices  8.66 us (5%)
  waiting for transfers between devices  6.54 us (4%)
    dot_general x3, matrix products, scatter_terms(): jnp.einsum(pattern, couplings, gathered, preferred_element_type=jnp.float32)  35.6 us
    gather x5, local copies, waits for them, and re-layouts, take_links(): member_col[:, member_links]  20.9 us
    psum x1, blocking collectives, body(): return lax.psum(local_green, 'energy')  20.3 us
    another operation x3, local copies, waits for them, and re-layouts  11.7 us
    reshape x1, local copies, waits for them, and re-layouts, solve_zones(): couplings = couplings_flat.reshape(e_dev, a_dev, Z, NB, 2, L, L)  11.6 us
    ppermute x3, starting transfers between devices, body(): from_right = lax.ppermute(from_right, 'atom', behind)  8.17 us
    ppermute x4, waiting for transfers between devices, body(): from_left = lax.ppermute(from_left, 'atom', right)  6.48 us
    add x3, other arithmetic, scatter_terms(): imag_part = products[..., 1, 0, :, :] + products[..., 0, 1, :, :]  5.8 us
  transfers between devices with their start and end apart: 7, of which 3 were waited for; matrix products, arithmetic and copies ran while one was open for 21% of the time, Pallas kernels for 0%

profile of v1, /device:TPU:0, one launch (start us, length us, event | category | flops | bytes accessed | tf_op | source)
XLA Modules:
  0.0 158.7 jit_solution(942247428644622184)
XLA Ops:
  0.5 2.9 %collective-permute-start.1 = (bf16[1,2,2048]{2,1,0:T(2,128)(2,1)}, bf16[1,2,2048]{2,1,0:T(2,128)(2,1)S(1)}, u32[]{:S(2)}, u32[]{:S(2)}) collective-permute-start(bf16[1,2,2048]{2,1,0:T(2,128)(2,1)} %param.9), channel_id=1, source_target_pairs={{0,7},{1,0},{2,1},{3,2},{4,3},{5,4},{6,5},{7,6},{8,15},{9,8},{10,9... | collective-permute-start | bytes 24584 | tf_op jit(solution)/shard_map/ppermute | solution.py:77
  7.0 1.4 fusion.58
  9.2 3.4 %gather_fusion.1 = bf16[768,2048]{1,0:T(8,128)(2,1)S(1)} fusion(bf16[64,2048]{1,0:T(8,128)(2,1)S(1)} %bitcast.164, s32[1024]{0:T(1024)S(1)} %pad_clamp_fusion), kind=kCustom, calls=%fused_computation.1 | custom fusion | bytes 6294528 | tf_op jit(solution)/shard_map/gather | solution.py:86
  12.7 11.7 %reshape.277 = bf16[2,64,6,2,32,32]{5,4,3,2,1,0:T(8,128)(2,1)} reshape(bf16[768,2048]{1,0:T(8,128)(2,1)S(1)} %gather_fusion.1) | data formatting | bytes 6291456 | tf_op jit(solution)/shard_map/reshape.48
  24.3 11.6 %reshape.280 = bf16[1,2,64,6,2,32,32]{6,5,4,3,2,1,0:T(8,128)(2,1)} reshape(bf16[768,2048]{1,0:T(8,128)(2,1)S(1)} %gather_fusion.1) | data formatting | bytes 6291456 | tf_op jit(solution)/shard_map/reshape | solution.py:37
  36.1 2.6 %collective-permute-start.3 = (bf16[1,2,2048]{2,1,0:T(2,128)(2,1)S(1)}, bf16[1,2,2048]{2,1,0:T(2,128)(2,1)S(1)}, u32[]{:S(2)}, u32[]{:S(2)}) collective-permute-start(bf16[1,2,2048]{2,1,0:T(2,128)(2,1)S(1)} %collective-permute-done.1), channel_id=1, source_target_pairs={{0,7},{1,0},{2,1},{3,2},{4,3},{5,4},{6,5},{7,6},{8,15},{9,8},{10,9... | collective-permute-start | bytes 24584 | tf_op jit(solution)/shard_map/ppermute | solution.py:77
  38.8 1.3 collective-permute-done.2
  40.1 2.6 %collective-permute-start.5 = (bf16[1,2,2048]{2,1,0:T(2,128)(2,1)S(1)}, bf16[1,2,2048]{2,1,0:T(2,128)(2,1)S(1)}, u32[]{:S(2)}, u32[]{:S(2)}) collective-permute-start(bf16[1,2,2048]{2,1,0:T(2,128)(2,1)S(1)} %collective-permute-done.3), channel_id=1, source_target_pairs={{0,7},{1,0},{2,1},{3,2},{4,3},{5,4},{6,5},{7,6},{8,15},{9,8},{10,9... | collective-permute-start | bytes 24584 | tf_op jit(solution)/shard_map/ppermute | solution.py:77
  42.8 1.3 collective-permute-done.4
  44.1 3.9 %collective-permute-done.6 = bf16[1,2,2048]{2,1,0:T(2,128)(2,1)S(1)} collective-permute-done((bf16[1,2,2048]{2,1,0:T(2,128)(2,1)S(1)}, bf16[1,2,2048]{2,1,0:T(2,128)(2,1)S(1)}, u32[]{:S(2)}, u32[]{:S(2)}) %collective-permute-start.6) | collective-permute-done | bytes 8224 | tf_op jit(solution)/shard_map/ppermute | solution.py:72
  49.7 2.0 %copy.45 = bf16[1,2,64,2,32,32]{5,4,2,1,3,0:T(8,128)(2,1)S(1)} copy(bf16[1,2,64,2,32,32]{2,1,5,4,3,0:T(2,128)(2,1)S(1)} %gather.18) | data formatting | bytes 1048576 | tf_op jit(solution)/shard_map/gather | solution.py:84
  52.4 1.2 maximum_maximum_fusion
  53.6 1.3 copy-done.2
  55.4 9.3 %gather_fusion.2 = bf16[768,2,32,32]{3,2,1,0:T(8,128)(2,1)} fusion(bf16[2,64,2,32,32]{4,3,2,1,0:T(8,128)(2,1)S(1)} %bitcast.165, s32[768]{0:T(1024)S(1)} %reshape.305), kind=kCustom, calls=%fused_computation.2 | custom fusion | bytes 6297600 | tf_op jit(solution)/shard_map/vmap()/gather | solution.py:30
  64.7 17.2 %fusion.6 = f32[1,2,64,2,2,32,32]{5,6,3,4,2,1,0:T(8,128)} fusion(bf16[2,64,6,2,32,32,1]{5,4,3,2,1,0,6:T(8,128)(2,1)} %bitcast.168, bf16[2,64,6,2,32,32]{5,4,3,2,1,0:T(8,128)(2,1)} %reshape.277), kind=kOutput, calls=%fused_computation.11 | convolution fusion | flops 201326592 | bytes 8388608 | tf_op jit(solution)/shard_map/eganpij,eganqjk->egapqik/dot_general | solution.py:22
  81.9 2.7 %fusion.27 = bf16[2,64,32,32]{2,3,1,0:T(8,128)(2,1)S(1)} fusion(f32[1,2,64,2,2,32,32]{5,6,3,4,2,1,0:T(8,128)} %fusion.6), kind=kLoop, calls=%fused_computation.34 | loop fusion | flops 262144 | bytes 1310720 | tf_op jit(solution)/shard_map/sub | solution.py:23
  84.7 2.9 %fusion.28 = bf16[2,64,32,32]{2,3,1,0:T(8,128)(2,1)S(1)} fusion(f32[1,2,64,2,2,32,32]{5,6,3,4,2,1,0:T(8,128)} %fusion.6), kind=kLoop, calls=%fused_computation.35 | loop fusion | flops 262144 | bytes 1310720 | tf_op jit(solution)/shard_map/add | solution.py:24
  87.6 1.3 fusion.24
  88.9 1.4 copy-done.5
  91.0 1.8 %convert_element_type.37 = bf16[1,2,64,64,32]{3,4,2,1,0:T(8,128)(2,1)S(1)} convert(f32[1,2,64,64,32]{3,4,2,1,0:T(8,128)} %constant_dynamic-update-slice_fusion.1) | non-fusion elementwise | flops 262144 | bytes 1572864 | tf_op jit(solution)/shard_map/convert_element_type | solution.py:42
  93.9 9.3 %gather_fusion.3 = bf16[768,2,32,32]{3,2,1,0:T(8,128)(2,1)} fusion(bf16[2,64,2,32,32]{4,3,2,1,0:T(8,128)(2,1)S(1)} %bitcast.166, s32[768]{0:T(1024)S(1)} %reshape.305), kind=kCustom, calls=%fused_computation.3 | custom fusion | bytes 6297600 | tf_op jit(solution)/shard_map/vmap()/gather | solution.py:30
  103.2 17.2 %fusion.11 = f32[1,2,64,2,2,32,32]{5,6,3,4,2,1,0:T(8,128)} fusion(bf16[2,64,6,2,32,32,1]{5,4,3,2,1,0,6:T(8,128)(2,1)} %bitcast.167, bf16[2,64,6,2,32,32]{5,4,3,2,1,0:T(8,128)(2,1)} %reshape.277), kind=kOutput, calls=%fused_computation.12 | convolution fusion | flops 201326592 | bytes 8388608 | tf_op jit(solution)/shard_map/eganpij,eganqjk->egapqik/dot_general | solution.py:22
  120.4 2.7 %fusion.29 = bf16[2,64,32,32]{2,3,1,0:T(8,128)(2,1)S(1)} fusion(f32[1,2,64,2,2,32,32]{5,6,3,4,2,1,0:T(8,128)} %fusion.11), kind=kLoop, calls=%fused_computation.36 | loop fusion | flops 262144 | bytes 1310720 | tf_op jit(solution)/shard_map/sub | solution.py:23
  123.2 2.9 %fusion.30 = bf16[2,64,32,32]{2,3,1,0:T(8,128)(2,1)S(1)} fusion(f32[1,2,64,2,2,32,32]{5,6,3,4,2,1,0:T(8,128)} %fusion.11), kind=kLoop, calls=%fused_computation.37 | loop fusion | flops 262144 | bytes 1310720 | tf_op jit(solution)/shard_map/add | solution.py:24
  126.1 1.3 fusion.22
  127.3 1.3 copy-done.6
  129.5 1.9 %convert_element_type.38 = bf16[1,2,64,64,32]{3,4,2,1,0:T(8,128)(2,1)S(1)} convert(f32[1,2,64,64,32]{3,4,2,1,0:T(8,128)} %constant_dynamic-update-slice_fusion) | non-fusion elementwise | flops 262144 | bytes 1572864 | tf_op jit(solution)/shard_map/convert_element_type | solution.py:51
  131.3 1.8 %copy.86 = bf16[1,2,64,64,32]{4,3,2,1,0:T(8,128)(2,1)} copy(bf16[1,2,64,64,32]{3,4,2,1,0:T(8,128)(2,1)S(1)} %convert_element_type.38) | data formatting | bytes 1048576 | tf_op jit(solution)/shard_map/vmap()/transpose;reshape | solution.py:30
  133.2 2.2 %gather_fusion.4 = bf16[12,2,32,32]{3,2,1,0:T(8,128)(2,1)S(1)} fusion(bf16[2,64,2,32,32]{4,3,2,1,0:T(8,128)(2,1)} %bitcast.171, s32[12]{0:T(128)S(1)} %reshape.321), kind=kCustom, calls=%fused_computation.4 | custom fusion | bytes 98400 | tf_op jit(solution)/shard_map/vmap()/gather | solution.py:30
  135.4 1.2 convolution_bitcast_fusion
  136.9 1.3 multiply_subtract_fusion
  138.4 20.3 %psum.7 = f32[2,2048]{1,0:T(2,128)} all-reduce(f32[2,2048]{1,0:T(2,128)S(1)} %pad_maximum_fusion), channel_id=1, replica_groups=mesh['energy'=4,'atom'=8] {'energy'}, use_global_device_ids=true, to_apply=%region_0.1 | all-reduce | flops 4096 | bytes 32768 | tf_op jit(solution)/shard_map/psum | solution.py:95
  (64 shorter events, 11.0 us)
Async XLA Ops:
  0.0 9.2 %copy-start = (bf16[1,64,2048]{2,1,0:T(8,128)(2,1)S(1)}, bf16[1,64,2048]{2,1,0:T(8,128)(2,1)}, u32[]{:S(2)}) copy-start(bf16[1,64,2048]{2,1,0:T(8,128)(2,1)} %param.10) | copy-start | bytes 786436
  0.0 36.1 %collective-permute-start = (bf16[1,2,2048]{2,1,0:T(2,128)(2,1)}, bf16[1,2,2048]{2,1,0:T(2,128)(2,1)S(1)}, u32[]{:S(2)}, u32[]{:S(2)}) collective-permute-start(bf16[1,2,2048]{2,1,0:T(2,128)(2,1)} %param.9), channel_id=1, source_target_pairs={{0,1},{1,2},{2,3},{3,4},{4,5},{5,6},{6,7},{7,0},{8,9},{9,10},{10,1... | collective-permute-start | bytes 24584 | tf_op jit(solution)/shard_map/ppermute | solution.py:72
  0.5 35.6 %collective-permute-start.1 = (bf16[1,2,2048]{2,1,0:T(2,128)(2,1)}, bf16[1,2,2048]{2,1,0:T(2,128)(2,1)S(1)}, u32[]{:S(2)}, u32[]{:S(2)}) collective-permute-start(bf16[1,2,2048]{2,1,0:T(2,128)(2,1)} %param.9), channel_id=1, source_target_pairs={{0,7},{1,0},{2,1},{3,2},{4,3},{5,4},{6,5},{7,6},{8,15},{9,8},{10,9... | collective-permute-start | bytes 24584 | tf_op jit(solution)/shard_map/ppermute | solution.py:77
  36.1 4.0 %collective-permute-start.2 = (bf16[1,2,2048]{2,1,0:T(2,128)(2,1)S(1)}, bf16[1,2,2048]{2,1,0:T(2,128)(2,1)S(1)}, u32[]{:S(2)}, u32[]{:S(2)}) collective-permute-start(bf16[1,2,2048]{2,1,0:T(2,128)(2,1)S(1)} %collective-permute-done), channel_id=1, source_target_pairs={{0,1},{1,2},{2,3},{3,4},{4,5},{5,6},{6,7},{7,0},{8,9},{9,10},{10,1... | collective-permute-start | bytes 24584 | tf_op jit(solution)/shard_map/ppermute | solution.py:72
  36.1 4.0 %collective-permute-start.3 = (bf16[1,2,2048]{2,1,0:T(2,128)(2,1)S(1)}, bf16[1,2,2048]{2,1,0:T(2,128)(2,1)S(1)}, u32[]{:S(2)}, u32[]{:S(2)}) collective-permute-start(bf16[1,2,2048]{2,1,0:T(2,128)(2,1)S(1)} %collective-permute-done.1), channel_id=1, source_target_pairs={{0,7},{1,0},{2,1},{3,2},{4,3},{5,4},{6,5},{7,6},{8,15},{9,8},{10,9... | collective-permute-start | bytes 24584 | tf_op jit(solution)/shard_map/ppermute | solution.py:77
  40.1 4.0 %collective-permute-start.4 = (bf16[1,2,2048]{2,1,0:T(2,128)(2,1)S(1)}, bf16[1,2,2048]{2,1,0:T(2,128)(2,1)S(1)}, u32[]{:S(2)}, u32[]{:S(2)}) collective-permute-start(bf16[1,2,2048]{2,1,0:T(2,128)(2,1)S(1)} %collective-permute-done.2), channel_id=1, source_target_pairs={{0,1},{1,2},{2,3},{3,4},{4,5},{5,6},{6,7},{7,0},{8,9},{9,10},{10,1... | collective-permute-start | bytes 24584 | tf_op jit(solution)/shard_map/ppermute | solution.py:72
  40.1 4.0 %collective-permute-start.5 = (bf16[1,2,2048]{2,1,0:T(2,128)(2,1)S(1)}, bf16[1,2,2048]{2,1,0:T(2,128)(2,1)S(1)}, u32[]{:S(2)}, u32[]{:S(2)}) collective-permute-start(bf16[1,2,2048]{2,1,0:T(2,128)(2,1)S(1)} %collective-permute-done.3), channel_id=1, source_target_pairs={{0,7},{1,0},{2,1},{3,2},{4,3},{5,4},{6,5},{7,6},{8,15},{9,8},{10,9... | collective-permute-start | bytes 24584 | tf_op jit(solution)/shard_map/ppermute | solution.py:77
  44.0 4.0 %collective-permute-start.6 = (bf16[1,2,2048]{2,1,0:T(2,128)(2,1)S(1)}, bf16[1,2,2048]{2,1,0:T(2,128)(2,1)S(1)}, u32[]{:S(2)}, u32[]{:S(2)}) collective-permute-start(bf16[1,2,2048]{2,1,0:T(2,128)(2,1)S(1)} %collective-permute-done.4), channel_id=1, source_target_pairs={{0,1},{1,2},{2,3},{3,4},{4,5},{5,6},{6,7},{7,0},{8,9},{9,10},{10,1... | collective-permute-start | bytes 24584 | tf_op jit(solution)/shard_map/ppermute | solution.py:72
  53.6 1.4 copy-start.2
  84.7 2.9 %copy-start.3 = (bf16[1,2,64,64,64]{4,3,2,1,0:T(8,128)(2,1)S(1)}, bf16[1,2,64,64,64]{4,3,2,1,0:T(8,128)(2,1)}, u32[]{:S(2)}) copy-start(bf16[1,2,64,64,64]{4,3,2,1,0:T(8,128)(2,1)} %copy-done.2) | copy-start | bytes 3145732
  88.9 1.4 copy-start.5
  123.2 2.9 %copy-start.4 = (bf16[1,2,64,64,64]{4,3,2,1,0:T(8,128)(2,1)S(1)}, bf16[1,2,64,64,64]{4,3,2,1,0:T(8,128)(2,1)}, u32[]{:S(2)}) copy-start(bf16[1,2,64,64,64]{4,3,2,1,0:T(8,128)(2,1)} %copy-done.2) | copy-start | bytes 3145732
  127.3 1.3 copy-start.6
  129.5 29.2 %copy-start.1 = (bf16[1,64,2048]{2,1,0:T(8,128)(2,1)S(1)}, bf16[1,64,2048]{2,1,0:T(8,128)(2,1)}, u32[]{:S(2)}) copy-start(bf16[1,64,2048]{2,1,0:T(8,128)(2,1)} %param.10) | copy-start | bytes 786436
